TPU v7x, 256 devices: a whole 4x4x8 slice. The times are simulated.
256 devices in a mesh: fsdp: 16 (over x, y), seq: 16 (over z, core).
Axes of the slice: x: 4, y: 4, z: 8, core: 2. Of those that a mesh axis runs over, the one named last changes fastest.
Arguments:
- tokens: bfloat16 [65536, 2048], P(('fsdp', 'seq')), may hold values from -6 to 6
- seq_lengths: int32 [16, 4], P('fsdp'), may hold values from 1 to 2048, 4096 in all within a row
- in_weight: bfloat16 [2048, 6144], P(None, 'fsdp'), may hold values from -0.125 to 0.125
- short_filter: float32 [7, 6144], replicated, may hold values from -2.5 to 2.5
- long_filter: bfloat16 [128, 128], replicated, may hold values from -0.5 to 0.5
- out_weight: bfloat16 [2048, 2048], replicated, may hold values from -0.125 to 0.125
Outputs:
- mixed: bfloat16 [65536, 2048], P(('fsdp', 'seq'))
Inputs may be any that keep to these rules, and one draw needn't show every extreme that they name: `seq_lengths`: in each pack the 4 lengths sum to 4096 and the longest is exactly 2048.
All inputs are finite; a program needn't handle non-finite values.
Results may differ from a plain program's by a relative error of at most 0.0073.
Values may be sent and summed in bfloat16 or wider, within the bound.
No kernel may reach another device: no remote copies, remote signals or barrier semaphores. Data moves between devices by JAX's collectives and lax.ppermute only.
A program may use at most 128 MiB of HBM per device.

v0:
```python
import jax
import jax.numpy as jnp
from jax import lax
from jax.sharding import PartitionSpec as P

LANE = 128
GROUP_DEVS = 4


def positions(row_ids, seq_starts):
    seq_begin = jnp.max(
        jnp.where(seq_starts[None, :] <= row_ids[:, None], seq_starts[None, :], 0), axis=1
    )
    return row_ids - seq_begin


def tap_table(tap_ids, long_filter):
    filter_len = long_filter.shape[0]
    one_hot = (
        tap_ids[:, :, None] == jnp.arange(filter_len, dtype=jnp.int32)[None, None, :]
    ).astype(jnp.bfloat16)
    return jnp.einsum(
        "ijt,tg->gij", one_hot, long_filter, preferred_element_type=jnp.float32
    ).astype(jnp.bfloat16)


def local(tokens, seq_lengths, in_weight, short_filter, long_filter, out_weight):
    rows, channels = tokens.shape
    width = short_filter.shape[0]
    filter_len, group_count = long_filter.shape
    per_group = channels // group_count
    n_seq = lax.axis_size("seq")
    s = lax.axis_index("seq")
    member = s % GROUP_DEVS
    part = LANE // GROUP_DEVS
    n_lblk = channels // LANE
    tail = filter_len + 8
    span = GROUP_DEVS * rows
    ext_rows = tail + span
    swaps = [[(i, i ^ d) for i in range(n_seq)] for d in range(1, GROUP_DEVS)]
    from_member = [tokens, lax.ppermute(tokens, "seq", swaps[0])]
    for d in range(2, GROUP_DEVS, 2):
        fetched = lax.ppermute(tokens, "seq", swaps[d - 1])
        from_member += [fetched, lax.ppermute(fetched, "seq", swaps[0])]
    blocks = []
    for m in range(GROUP_DEVS):
        pick = from_member[0]
        for d in range(1, GROUP_DEVS):
            pick = jnp.where(member ^ d == m, from_member[d], pick)
        blocks.append(pick)
    tail_src = tokens[rows - tail :]
    tail_tok = jnp.zeros_like(tail_src)
    for m in range(GROUP_DEVS):
        dist = m + 1
        perm = [(i - dist, i) for i in range(GROUP_DEVS, n_seq) if i % GROUP_DEVS == m]
        got = lax.ppermute(tail_src, "seq", perm)
        tail_tok = jnp.where(member == m, got, tail_tok)
    ext_tokens = jnp.concatenate([tail_tok] + blocks, axis=0)
    lengths_row = seq_lengths[0]
    seq_starts = jnp.cumsum(lengths_row) - lengths_row
    pair_start = s // GROUP_DEVS * span
    row_ids = pair_start - tail + jnp.arange(ext_rows, dtype=jnp.int32)
    position = positions(row_ids, seq_starts)
    offset = member * part
    w_t = in_weight.T.reshape(in_weight.shape[1] // LANE, LANE, channels)
    w_part = lax.dynamic_slice_in_dim(w_t, offset, part, axis=1)
    w_all = lax.all_gather(w_part, "fsdp", axis=0, tiled=True)
    own = n_lblk * part
    w_all = w_all.reshape(3 * own, channels)
    ow = out_weight.reshape(n_lblk, LANE, channels)
    weights = []
    for d in range(GROUP_DEVS):
        src_offset = (member ^ d) * part
        weights.append(
            lax.dynamic_slice_in_dim(ow, src_offset, part, axis=1).reshape(own, channels)
        )
    ow_cat = jnp.concatenate(weights, axis=0)
    ext_tokens, ow_cat = lax.optimization_barrier((ext_tokens, ow_cat))
    projected = jnp.dot(ext_tokens, w_all.T, preferred_element_type=jnp.float32).astype(
        jnp.bfloat16
    )
    taps = short_filter.reshape(width, 3, n_lblk, LANE)
    taps = lax.dynamic_slice_in_dim(taps, offset, part, axis=3).reshape(width, 3 * own)
    start = 8
    feat_rows = ext_rows - start
    pos_f = position[start:]
    featured = jnp.zeros((feat_rows, 3 * own), jnp.float32)
    for tap_index in range(width):
        shifted = projected[start - tap_index : ext_rows - tap_index].astype(jnp.float32)
        featured = featured + taps[tap_index] * jnp.where(
            (pos_f >= tap_index)[:, None], shifted, 0.0
        )
    queries = featured[feat_rows - span :, :own]
    mixed_in = (featured[:, own : 2 * own] * featured[:, 2 * own :]).astype(jnp.bfloat16)
    sub = LANE // per_group
    lf = long_filter.reshape(filter_len, n_lblk, sub)
    lf = lax.dynamic_slice_in_dim(lf, offset // per_group, part // per_group, axis=2)
    lf = lf.reshape(filter_len, own // per_group)
    n_groups = own // per_group
    out_rows = jnp.arange(filter_len, dtype=jnp.int32)[:, None]
    src_rows = jnp.arange(filter_len, dtype=jnp.int32)[None, :]
    cur_tap = out_rows - src_rows
    prev_tap = out_rows + filter_len - src_rows
    cur_table = tap_table(cur_tap, lf)
    prev_table = tap_table(prev_tap, lf)
    n_blocks = span // filter_len
    pos_out = position[tail:].reshape(n_blocks, filter_len)
    cur_kernel = jnp.where(
        (cur_tap[None] <= pos_out[:, :, None])[:, None], cur_table[None], 0.0
    ).astype(jnp.bfloat16)
    prev_kernel = jnp.where(
        (prev_tap[None] <= pos_out[:, :, None])[:, None], prev_table[None], 0.0
    ).astype(jnp.bfloat16)
    mi_t = mixed_in.T.reshape(n_groups, per_group, n_blocks + 1, filter_len)
    filtered = jnp.einsum(
        "gcbj,bgij->gcbi", mi_t[:, :, 1:], cur_kernel, preferred_element_type=jnp.float32
    )
    filtered = filtered + jnp.einsum(
        "gcbj,bgij->gcbi", mi_t[:, :, :-1], prev_kernel, preferred_element_type=jnp.float32
    )
    filtered = filtered.reshape(own, span)
    gated = (queries.T * filtered).astype(jnp.bfloat16)
    gated = gated.T.reshape(GROUP_DEVS, rows, own)
    pieces = []
    for d in range(GROUP_DEVS):
        send = lax.dynamic_index_in_dim(gated, member ^ d, axis=0, keepdims=False)
        got = send if d == 0 else lax.ppermute(send, "seq", swaps[d - 1])
        pieces.append(got)
    result = tokens.astype(jnp.float32) + jnp.dot(
        jnp.concatenate(pieces, axis=1), ow_cat, preferred_element_type=jnp.float32
    )
    return result.astype(jnp.bfloat16)


def solution(mesh):
    in_specs = (P(("fsdp", "seq"), None), P("fsdp", None), P(None, "fsdp"), P(), P(), P())
    out_specs = P(("fsdp", "seq"), None)
    return jax.shard_map(local, mesh=mesh, in_specs=in_specs, out_specs=out_specs, check_vma=False)
```

profile of v0, /device:TPU:1, one launch (start us, length us, event | category | flops | bytes accessed | tf_op | source)
XLA Modules:
  0.0 154.7 jit_solution(10799367417863991124)
XLA Ops:
  6.5 1.8 %copy.26 = bf16[2048,384]{0,1:T(8,128)(2,1)S(1)} copy(bf16[2048,384]{1,0:T(8,128)(2,1)} %param.8) | data formatting | bytes 3145728 | tf_op args[2]
  9.2 1.1 slice.75
  11.0 1.5 collective-permute-start.1
  12.4 1.5 collective-permute-start.2
  13.9 1.5 collective-permute-start.3
  15.4 8.6 %collective-permute-start.4 = (bf16[256,2048]{1,0:T(8,128)(2,1)S(1)}, bf16[256,2048]{1,0:T(8,128)(2,1)S(1)}, u32[]{:S(2)}, u32[]{:S(2)}) collective-permute-start(bf16[256,2048]{1,0:T(8,128)(2,1)S(1)} %copy-done.1), channel_id=1, source_target_pairs={{0,2},{1,3},{2,0},{3,1},{4,6},{5,7},{6,4},{7,5},{8,10},{9,11},{10,... | collective-permute-start | bytes 3145736 | tf_op jit(solution)/shard_map/ppermute | solution.py:43
  27.4 4.0 %fusion.20 = bf16[32,128,128]{2,0,1:T(8,128)(2,1)S(1)} fusion(bf16[128,32,1]{0,1,2:T(8,128)(2,1)S(1)} %bitcast.77, s32[128,128]{1,0:T(8,128)S(1)} %get-tuple-element.35), kind=kOutput, calls=%fused_computation.28 | convolution fusion | flops 136839168 | bytes 1122304 | tf_op jit(solution)/shard_map/ijt,tg->gij/dot_general | solution.py:22
  31.4 1.4 copy.31
  32.8 3.9 %fusion.21 = bf16[32,128,128]{2,0,1:T(8,128)(2,1)S(1)} fusion(bf16[128,32,1]{0,1,2:T(8,128)(2,1)S(1)} %bitcast.78, s32[128,128]{1,0:T(8,128)S(1)} %get-tuple-element.36), kind=kOutput, calls=%fused_computation.29 | convolution fusion | flops 136839168 | bytes 1122304 | tf_op jit(solution)/shard_map/ijt,tg->gij/dot_general | solution.py:22
  36.7 1.4 copy.28
  39.2 4.3 %constant_dynamic-slice_fusion.11 = (bf16[16,32,2048]{2,1,0:T(8,128)(2,1)S(1)}, bf16[16,32,2048]{2,1,0:T(8,128)(2,1)S(1)}, bf16[16,32,2048]{2,1,0:T(8,128)(2,1)S(1)}, bf16[16,32,2048]{2,1,0:T(8,128)(2,1)S(1)}) fusion(bf16[16,128,2048]{2,1,0:T(8,128)(2,1)} %bitcast.65, s32[]{:T(128)S(6)} %select_n.178, s32[]{:T(128)S(6)} %select_n.215, s32[]{:T(128)S(6)} %select_n.214, ...), kind=kLoop, calls=%fused_computation.73 | loop fusion | bytes 16777232 | tf_op jit(solution)/shard_map/dynamic_slice | solution.py:75
  44.2 4.1 %pad_maximum_fusion = bf16[2048,2048]{1,0:T(8,128)(2,1)} fusion(bf16[512,2048]{1,0:T(8,128)(2,1)S(1)} %bitcast.69, bf16[512,2048]{1,0:T(8,128)(2,1)S(1)} %bitcast.70, bf16[512,2048]{1,0:T(8,128)(2,1)S(1)} %bitcast.71, bf16[512,2048]{1,0:T(8,128)(2,1)S(1)} %bitcast.68), kind=kLoop, calls=%fused_computation | loop fusion | flops 33554432 | bytes 16777216 | tf_op jit(solution)/shard_map/concatenate | solution.py:77
  48.3 2.3 %select_dynamic-update-slice_fusion.4 = bf16[1160,2048]{1,0:T(8,128)(2,1)} fusion(bf16[136,2048]{1,0:T(8,128)(2,1)S(1)} %collective-permute-done, bf16[136,2048]{1,0:T(8,128)(2,1)} %collective-permute-done.1, bf16[136,2048]{1,0:T(8,128)(2,1)} %collective-permute-done.2, bf16[136,2048]{1,0:T(8,128)(2,1)} %collective-permute-done.3, pred[]{:T(512)S(6)} %eq.79, ...), kind=kLoop, calls=%fused_computation.44 | loop fusion | flops 1114111 | bytes 2785284
  50.6 1.7 %select_dynamic-update-slice_fusion.3 = bf16[1160,2048]{1,0:T(8,128)(2,1)} fusion(bf16[1160,2048]{1,0:T(8,128)(2,1)} %select_dynamic-update-slice_fusion.4, bf16[256,2048]{1,0:T(8,128)(2,1)S(1)} %collective-permute-done.5, bf16[256,2048]{1,0:T(8,128)(2,1)S(1)} %collective-permute-done.4, bf16[256,2048]{1,0:T(8,128)(2,1)S(1)} %collective-permute-done.6, ...), kind=kLoop, calls=%fused_computation.43 | loop fusion | flops 1572864 | bytes 5242883
  52.3 1.7 %select_dynamic-update-slice_fusion.2 = bf16[1160,2048]{1,0:T(8,128)(2,1)} fusion(bf16[1160,2048]{1,0:T(8,128)(2,1)} %select_dynamic-update-slice_fusion.3, bf16[256,2048]{1,0:T(8,128)(2,1)S(1)} %collective-permute-done.5, bf16[256,2048]{1,0:T(8,128)(2,1)S(1)} %collective-permute-done.4, bf16[256,2048]{1,0:T(8,128)(2,1)S(1)} %collective-permute-done.6, ...), kind=kLoop, calls=%fused_computation.42 | loop fusion | flops 1572864 | bytes 5242883
  54.0 1.7 %select_dynamic-update-slice_fusion.1 = bf16[1160,2048]{1,0:T(8,128)(2,1)} fusion(bf16[1160,2048]{1,0:T(8,128)(2,1)} %select_dynamic-update-slice_fusion.2, bf16[256,2048]{1,0:T(8,128)(2,1)S(1)} %collective-permute-done.5, bf16[256,2048]{1,0:T(8,128)(2,1)S(1)} %collective-permute-done.4, bf16[256,2048]{1,0:T(8,128)(2,1)S(1)} %collective-permute-done.6, ...), kind=kLoop, calls=%fused_computation.41 | loop fusion | flops 1572864 | bytes 5242883
  55.7 1.7 %select_dynamic-update-slice_fusion = bf16[1160,2048]{1,0:T(8,128)(2,1)} fusion(bf16[1160,2048]{1,0:T(8,128)(2,1)} %select_dynamic-update-slice_fusion.1, bf16[256,2048]{1,0:T(8,128)(2,1)S(1)} %collective-permute-done.5, bf16[256,2048]{1,0:T(8,128)(2,1)S(1)} %collective-permute-done.4, bf16[256,2048]{1,0:T(8,128)(2,1)S(1)} %collective-permute-done.6, ...), kind=kLoop, calls=%fused_computation.40 | loop fusion | flops 1572864 | bytes 5242883 | tf_op jit(solution)/shard_map/concatenate | solution.py:58
  57.4 22.7 %all-gather.2.cloned.1.call-done = bf16[48,32,2048]{2,1,0:T(8,128)(2,1)} async-done(((bf16[3,32,2048]{2,1,0:T(8,128)(2,1)}), bf16[48,32,2048]{2,1,0:T(8,128)(2,1)}) %all-gather.2.cloned.1.call-update) | async-done | bytes 6291472 | tf_op jit(solution)/shard_map/all_gather | solution.py:67
  80.1 11.2 %convolution_convert_fusion = bf16[1160,1536]{1,0:T(8,128)(2,1)S(1)} fusion(bf16[1160,2048]{1,0:T(8,128)(2,1)} %select_dynamic-update-slice_fusion, bf16[1536,2048]{1,0:T(8,128)(2,1)} %bitcast.79), kind=kOutput, calls=%fused_computation.11 | convolution fusion | flops 7299870720 | bytes 14606336 | tf_op jit(solution)/shard_map/dot_general | solution.py:79
  91.2 10.7 %multiply_add_fusion = f32[1152,1536]{1,0:T(8,128)S(1)} fusion(bf16[1160,1536]{1,0:T(8,128)(2,1)S(1)} %convolution_convert_fusion, f32[1536]{0:T(1024)S(1)} %mul.115, f32[1536]{0:T(1024)S(1)} %mul.112, f32[1536]{0:T(1024)S(1)} %mul.109, f32[1536]{0:T(1024)S(1)} %mul.106, f32[1536]{0:T(1024)S(1)} %mul.103, f32[1536]{0:T(1024)S(1)} %mul.100, ...), kind=kLoop, calls=%fused_computation.12 | loop fusion | flops 47775744 | bytes 31901568 | tf_op jit(solution)/shard_map/add | solution.py:90
  101.9 2.9 %copy-done = f32[1152,1536]{1,0:T(8,128)} copy-done((f32[1152,1536]{1,0:T(8,128)}, f32[1152,1536]{1,0:T(8,128)S(1)}, u32[]{:S(2)}) %copy-start) | copy-done | bytes 7077912
  105.3 1.4 copy.29
  106.7 2.7 %reshape.154 = bf16[32,16,9,128]{3,2,1,0:T(8,128)(2,1)S(1)} reshape(bf16[512,1152]{1,0:T(8,128)(2,1)} %copy.29) | data formatting | bytes 2359296 | tf_op jit(solution)/shard_map/reshape | solution.py:114
  109.9 5.8 %fusion = f32[32,8,128,16]{2,3,1,0:T(8,128)S(1)} fusion(pred[8,128,128]{2,1,0:T(8,128)(4,1)S(1)} %copy-done.3, bf16[32,128,128]{2,1,0:T(8,128)(2,1)} %copy.31, bf16[32,16,8,128]{3,2,1,0:T(8,128)(2,1)S(1)} %get-tuple-element.14), kind=kOutput, calls=%fused_computation.1 | convolution fusion | flops 138412032 | bytes 4325376 | tf_op jit(solution)/shard_map/gcbj,bgij->gcbi/dot_general | solution.py:118
  115.6 4.5 %add_bitcast_fusion = f32[32,16,8,128]{3,1,2,0:T(8,128)S(1)} fusion(f32[32,8,128,16]{2,3,1,0:T(8,128)S(1)} %fusion, pred[8,128,128]{2,1,0:T(8,128)(4,1)S(1)} %get-tuple-element.33, bf16[32,128,128]{2,1,0:T(8,128)(2,1)S(1)} %copy-done.2, bf16[32,16,8,128]{3,2,1,0:T(8,128)(2,1)S(1)} %get-tuple-element.13), kind=kOutput, calls=%fused_computation.27 | convolution fusion | flops 138936320 | bytes 6422528 | tf_op jit(solution)/shard_map/gcbj,bgij->gcbi/dot_general | solution.py:115
  121.0 1.8 %copy.44 = f32[64,8,8,128]{3,1,2,0:T(8,128)} copy(f32[64,8,8,128]{3,2,1,0:T(8,128)S(1)} %bitcast.66) | data formatting | bytes 4194304
  122.8 1.9 %copy.34 = f32[512,1024]{0,1:T(8,128)S(1)} copy(f32[512,1024]{1,0:T(8,128)} %bitcast.67) | data formatting | bytes 4194304 | tf_op jit(solution)/shard_map/reshape | solution.py:121
  124.7 1.9 %fusion.17 = bf16[512,1024]{0,1:T(8,128)(2,1)S(1)} fusion(f32[512,1024]{0,1:T(8,128)S(1)} %copy.34, f32[1152,1536]{1,0:T(8,128)} %copy-done), kind=kLoop, calls=%fused_computation.26 | loop fusion | flops 1048576 | bytes 5242880 | tf_op jit(solution)/shard_map/convert_element_type | solution.py:122
  127.5 1.3 collective-permute-start.8
  129.2 6.1 %collective-permute-done.8 = bf16[256,512]{1,0:T(8,128)(2,1)S(1)} collective-permute-done((bf16[256,512]{1,0:T(8,128)(2,1)S(1)}, bf16[256,512]{1,0:T(8,128)(2,1)S(1)}, u32[]{:S(2)}, u32[]{:S(2)}) %collective-permute-start.8) | collective-permute-done | bytes 262176 | tf_op jit(solution)/shard_map/ppermute | solution.py:127
  135.4 5.8 %collective-permute-done.9 = bf16[256,512]{1,0:T(8,128)(2,1)S(1)} collective-permute-done((bf16[256,512]{1,0:T(8,128)(2,1)S(1)}, bf16[256,512]{1,0:T(8,128)(2,1)S(1)}, u32[]{:S(2)}, u32[]{:S(2)}) %collective-permute-start.9) | collective-permute-done | bytes 262176 | tf_op jit(solution)/shard_map/ppermute | solution.py:127
  141.2 6.7 %fusion.14 = bf16[256,2048]{1,0:T(8,128)(2,1)} fusion(bf16[2048,2048]{1,0:T(8,128)(2,1)} %pad_maximum_fusion, bf16[256,2048]{1,0:T(8,128)(2,1)S(1)} %copy-done.1, bf16[256,512]{1,0:T(8,128)(2,1)S(1)} %collective-permute-done.9, bf16[256,512]{1,0:T(8,128)(2,1)S(1)} %collective-permute-done.8, bf16[256,512]{1,0:T(8,128)(2,1)S(1)} %collective-permute-done.7, ...), kind=kOutput, calls=%fused_computation.20 | convolution fusion | flops 2153250816 | bytes 11534336 | tf_op jit(solution)/shard_map/dot_general | solution.py:129
  (50 shorter events, 9.7 us)
Async XLA Ops:
  6.5 8.8 %copy-start.1 = (bf16[256,2048]{1,0:T(8,128)(2,1)S(1)}, bf16[256,2048]{1,0:T(8,128)(2,1)}, u32[]{:S(2)}) copy-start(bf16[256,2048]{1,0:T(8,128)(2,1)} %param.6) | copy-start | bytes 3145732
  6.5 73.5 %all-gather.2.cloned.1.call-start = ((), (), s32[]{:S(2)}) async-start(), calls=%async_computation | async-start | bytes 6684672 | tf_op jit(solution)/shard_map/all_gather | solution.py:67
  10.3 33.3 %collective-permute-start = (bf16[136,2048]{1,0:T(8,128)(2,1)S(1)}, bf16[136,2048]{1,0:T(8,128)(2,1)S(1)}, u32[]{:S(2)}, u32[]{:S(2)}) collective-permute-start(bf16[136,2048]{1,0:T(8,128)(2,1)S(1)} %slice.75), channel_id=1, source_target_pairs={{3,7},{7,11},{11,15},{19,23},{23,27},{27,31},{35,39},{39,43},{43,4... | collective-permute-start | bytes 1671176 | tf_op jit(solution)/shard_map/ppermute | solution.py:56
  11.0 37.3 %collective-permute-start.1 = (bf16[136,2048]{1,0:T(8,128)(2,1)S(1)}, bf16[136,2048]{1,0:T(8,128)(2,1)}, u32[]{:S(2)}, u32[]{:S(2)}) collective-permute-start(bf16[136,2048]{1,0:T(8,128)(2,1)S(1)} %slice.75), channel_id=1, source_target_pairs={{3,6},{7,10},{11,14},{19,22},{23,26},{27,30},{35,38},{39,42},{43,4... | collective-permute-start | bytes 1671176 | tf_op jit(solution)/shard_map/ppermute | solution.py:56
  12.4 35.8 %collective-permute-start.2 = (bf16[136,2048]{1,0:T(8,128)(2,1)S(1)}, bf16[136,2048]{1,0:T(8,128)(2,1)}, u32[]{:S(2)}, u32[]{:S(2)}) collective-permute-start(bf16[136,2048]{1,0:T(8,128)(2,1)S(1)} %slice.75), channel_id=1, source_target_pairs={{3,5},{7,9},{11,13},{19,21},{23,25},{27,29},{35,37},{39,41},{43,45... | collective-permute-start | bytes 1671176 | tf_op jit(solution)/shard_map/ppermute | solution.py:56
  13.9 34.4 %collective-permute-start.3 = (bf16[136,2048]{1,0:T(8,128)(2,1)S(1)}, bf16[136,2048]{1,0:T(8,128)(2,1)}, u32[]{:S(2)}, u32[]{:S(2)}) collective-permute-start(bf16[136,2048]{1,0:T(8,128)(2,1)S(1)} %slice.75), channel_id=1, source_target_pairs={{3,4},{7,8},{11,12},{19,20},{23,24},{27,28},{35,36},{39,40},{43,44... | collective-permute-start | bytes 1671176 | tf_op jit(solution)/shard_map/ppermute | solution.py:56
  15.4 28.6 %collective-permute-start.4 = (bf16[256,2048]{1,0:T(8,128)(2,1)S(1)}, bf16[256,2048]{1,0:T(8,128)(2,1)S(1)}, u32[]{:S(2)}, u32[]{:S(2)}) collective-permute-start(bf16[256,2048]{1,0:T(8,128)(2,1)S(1)} %copy-done.1), channel_id=1, source_target_pairs={{0,2},{1,3},{2,0},{3,1},{4,6},{5,7},{6,4},{7,5},{8,10},{9,11},{10,... | collective-permute-start | bytes 3145736 | tf_op jit(solution)/shard_map/ppermute | solution.py:43
  25.5 12.6 %copy-start.4 = (s32[1,4]{1,0:T(1,128)S(1)}, s32[1,4]{1,0:T(1,128)}, u32[]{:S(2)}) copy-start(s32[1,4]{1,0:T(1,128)} %param.7) | copy-start | bytes 52
  43.6 7.0 %collective-permute-start.6 = (bf16[256,2048]{1,0:T(8,128)(2,1)S(1)}, bf16[256,2048]{1,0:T(8,128)(2,1)S(1)}, u32[]{:S(2)}, u32[]{:S(2)}) collective-permute-start(bf16[256,2048]{1,0:T(8,128)(2,1)S(1)} %copy-done.1), channel_id=1, source_target_pairs={{0,1},{1,0},{2,3},{3,2},{4,5},{5,4},{6,7},{7,6},{8,9},{9,8},{10,11... | collective-permute-start | bytes 3145736 | tf_op jit(solution)/shard_map/ppermute | solution.py:41
  44.0 6.6 %collective-permute-start.5 = (bf16[256,2048]{1,0:T(8,128)(2,1)S(1)}, bf16[256,2048]{1,0:T(8,128)(2,1)S(1)}, u32[]{:S(2)}, u32[]{:S(2)}) collective-permute-start(bf16[256,2048]{1,0:T(8,128)(2,1)S(1)} %collective-permute-done.4), channel_id=1, source_target_pairs={{0,1},{1,0},{2,3},{3,2},{4,5},{5,4},{6,7},{7,6},{8,9},{9,8},{10,11... | collective-permute-start | bytes 3145736 | tf_op jit(solution)/shard_map/ppermute | solution.py:44
  101.9 2.9 %copy-start = (f32[1152,1536]{1,0:T(8,128)}, f32[1152,1536]{1,0:T(8,128)S(1)}, u32[]{:S(2)}) copy-start(f32[1152,1536]{1,0:T(8,128)S(1)} %multiply_add_fusion) | copy-start | bytes 21233668
  105.3 4.6 %copy-start.3 = (pred[8,128,128]{2,1,0:T(8,128)(4,1)S(1)}, pred[8,128,128]{2,1,0:T(8,128)(4,1)}, u32[]{:S(2)}) copy-start(pred[8,128,128]{2,1,0:T(8,128)(4,1)} %get-tuple-element.34) | copy-start | bytes 393220
  109.9 5.8 %copy-start.2 = (bf16[32,128,128]{2,1,0:T(8,128)(2,1)S(1)}, bf16[32,128,128]{2,1,0:T(8,128)(2,1)}, u32[]{:S(2)}) copy-start(bf16[32,128,128]{2,1,0:T(8,128)(2,1)} %copy.28) | copy-start | bytes 3145732
  126.7 2.5 %collective-permute-start.7 = (bf16[256,512]{1,0:T(8,128)(2,1)S(1)}, bf16[256,512]{1,0:T(8,128)(2,1)S(1)}, u32[]{:S(2)}, u32[]{:S(2)}) collective-permute-start(bf16[256,512]{1,0:T(8,128)(2,1)S(1)} %get-tuple-element.18), channel_id=1, source_target_pairs={{0,1},{1,0},{2,3},{3,2},{4,5},{5,4},{6,7},{7,6},{8,9},{9,8},{10,11... | collective-permute-start | bytes 786440 | tf_op jit(solution)/shard_map/ppermute | solution.py:127
  127.5 7.9 %collective-permute-start.8 = (bf16[256,512]{1,0:T(8,128)(2,1)S(1)}, bf16[256,512]{1,0:T(8,128)(2,1)S(1)}, u32[]{:S(2)}, u32[]{:S(2)}) collective-permute-start(bf16[256,512]{1,0:T(8,128)(2,1)S(1)} %get-tuple-element.17), channel_id=1, source_target_pairs={{0,2},{1,3},{2,0},{3,1},{4,6},{5,7},{6,4},{7,5},{8,10},{9,11},{10,... | collective-permute-start | bytes 786440 | tf_op jit(solution)/shard_map/ppermute | solution.py:127
  128.8 12.4 %collective-permute-start.9 = (bf16[256,512]{1,0:T(8,128)(2,1)S(1)}, bf16[256,512]{1,0:T(8,128)(2,1)S(1)}, u32[]{:S(2)}, u32[]{:S(2)}) collective-permute-start(bf16[256,512]{1,0:T(8,128)(2,1)S(1)} %get-tuple-element.16), channel_id=1, source_target_pairs={{0,3},{1,2},{2,1},{3,0},{4,7},{5,6},{6,5},{7,4},{8,11},{9,10},{10,... | collective-permute-start | bytes 786440 | tf_op jit(solution)/shard_map/ppermute | solution.py:127
Sparse Core Ops, SparseCore 0:
  9.8 70.1 all-gather.1
where the time goes:
time: 155 us
  matrix products  36 us (23%)
  waiting for transfers between devices  34.9 us (23%)
  other arithmetic  28.2 us (18%)
  local copies, waits for them, and re-layouts  25.5 us (16%)
  starting transfers between devices  16.5 us (11%)
  between operations  13.6 us (9%)
    all_gather x1, waiting for transfers between devices, local(): w_all = lax.all_gather(w_part, 'fsdp', axis=0, tiled=True)  22.7 us
    ppermute x3, waiting for transfers between devices, local(): got = send if d == 0 else lax.ppermute(send, 'seq', swaps[d - 1])  11.9 us
    dot_general x1, matrix products, local(): jnp.dot(ext_tokens, w_all.T, preferred_element_type=jnp.float32)  11.2 us
    add x1, other arithmetic, local(): featured + taps[tap_index] * jnp.where((pos_f >= tap_index)[:, None], shi...  10.7 us
    ppermute x1, starting transfers between devices, local(): fetched = lax.ppermute(tokens, 'seq', swaps[d - 1])  8.59 us
    unnamed x14, local copies, waits for them, and re-layouts  8.3 us
    dot_general x2, matrix products, tap_table(): jnp.einsum('ijt,tg->gij', one_hot, long_filter, preferred_element_type=jn...  7.92 us
    unnamed x4, other arithmetic  7.39 us
  transfers between devices with their start and end apart: 11, of which 4 were waited for; matrix products, arithmetic and copies ran while one was open for 22% of the time, Pallas kernels for 0%

commit v1 on v0

--- a/solution.py
+++ b/solution.py
@@ -64,7 +64,15 @@
     offset = member * part
     w_t = in_weight.T.reshape(in_weight.shape[1] // LANE, LANE, channels)
     w_part = lax.dynamic_slice_in_dim(w_t, offset, part, axis=1)
-    w_all = lax.all_gather(w_part, "fsdp", axis=0, tiled=True)
+
+    def digits_write(sample, row_dim, group_axis):
+        part_next = jnp.concatenate(lax.axis_size(group_axis) * [sample], axis=row_dim)
+        mixed_arr = lax.all_to_all(
+            part_next, axis_name=group_axis, split_axis=row_dim, concat_axis=row_dim, tiled=True
+        )
+        return mixed_arr
+
+    w_all = digits_write(w_part, 0, "fsdp")
     own = n_lblk * part
     w_all = w_all.reshape(3 * own, channels)
     ow = out_weight.reshape(n_lblk, LANE, channels)

time: 155 us -> 213 us (1.37)
  the two profiles are of different devices: /device:TPU:1 before, /device:TPU:221 now
where the time goes in v1:
time: 213 us
  waiting for transfers between devices  92 us (43%)
  local copies, waits for them, and re-layouts  38.3 us (18%)
  matrix products  36 us (17%)
  other arithmetic  28.5 us (13%)
  starting transfers between devices  17.4 us (8%)
    all_to_all x1, waiting for transfers between devices, digits_write(): lax.all_to_all(part_next, axis_name=group_axis, split_axis=row_dim, conca...  80.1 us
    unnamed x31, local copies, waits for them, and re-layouts  18.3 us
    ppermute x3, waiting for transfers between devices, local(): got = send if d == 0 else lax.ppermute(send, 'seq', swaps[d - 1])  11.9 us
    dot_general x1, matrix products, local(): jnp.dot(ext_tokens, w_all.T, preferred_element_type=jnp.float32)  11.2 us
    add x1, other arithmetic, local(): featured + taps[tap_index] * jnp.where((pos_f >= tap_index)[:, None], shi...  10.7 us
    dot_general x2, matrix products, tap_table(): jnp.einsum('ijt,tg->gij', one_hot, long_filter, preferred_element_type=jn...  7.91 us
    unnamed x4, other arithmetic  7.36 us
    all_to_all x1, starting transfers between devices, digits_write(): lax.all_to_all(part_next, axis_name=group_axis, split_axis=row_dim, conca...  6.68 us
  transfers between devices with their start and end apart: 11, of which 3 were waited for; matrix products, arithmetic and copies ran while one was open for 21% of the time, Pallas kernels for 0%

profile of v1, /device:TPU:221, one launch (start us, length us, event | category | flops | bytes accessed | tf_op | source)
XLA Modules:
  0.0 212.6 jit_solution(9981759015373712816)
XLA Ops:
  0.0 1.9 slice.75
  2.6 1.5 collective-permute-start.1
  5.4 1.5 collective-permute-start.3
  6.9 1.5 collective-permute-start.4
  8.4 1.7 copy.17
  22.6 6.7 %all-to-all-start = ((bf16[48,32,2048]{2,1,0:T(8,128)(2,1)}), bf16[48,32,2048]{2,1,0:T(8,128)(2,1)}, u32[]{:S(2)}, u32[]{:S(2)}) async-start(bf16[48,32,2048]{2,1,0:T(8,128)(2,1)} %constant_dynamic-update-slice_fusion), calls=%async_computation | async-start | bytes 12582912 | tf_op jit(solution)/shard_map/all_to_all | solution.py:70
  30.4 4.0 %fusion.20 = bf16[32,128,128]{2,0,1:T(8,128)(2,1)S(1)} fusion(bf16[128,32,1]{0,1,2:T(8,128)(2,1)S(1)} %bitcast.92, s32[128,128]{1,0:T(8,128)S(1)} %get-tuple-element.35), kind=kOutput, calls=%fused_computation.28 | convolution fusion | flops 136839168 | bytes 1122304 | tf_op jit(solution)/shard_map/ijt,tg->gij/dot_general | solution.py:22
  35.8 3.9 %fusion.21 = bf16[32,128,128]{2,0,1:T(8,128)(2,1)S(1)} fusion(bf16[128,32,1]{0,1,2:T(8,128)(2,1)S(1)} %bitcast.93, s32[128,128]{1,0:T(8,128)S(1)} %get-tuple-element.36), kind=kOutput, calls=%fused_computation.29 | convolution fusion | flops 136839168 | bytes 1122304 | tf_op jit(solution)/shard_map/ijt,tg->gij/dot_general | solution.py:22
  41.6 4.4 %constant_dynamic-slice_fusion.11 = (bf16[16,32,2048]{2,1,0:T(8,128)(2,1)S(1)}, bf16[16,32,2048]{2,1,0:T(8,128)(2,1)S(1)}, bf16[16,32,2048]{2,1,0:T(8,128)(2,1)S(1)}, bf16[16,32,2048]{2,1,0:T(8,128)(2,1)S(1)}) fusion(bf16[16,128,2048]{2,1,0:T(8,128)(2,1)} %bitcast.81, s32[]{:T(128)S(6)} %select_n.178, s32[]{:T(128)S(6)} %select_n.215, s32[]{:T(128)S(6)} %select_n.214, ...), kind=kLoop, calls=%fused_computation.89 | loop fusion | bytes 16777232 | tf_op jit(solution)/shard_map/dynamic_slice | solution.py:83
  47.1 4.1 %pad_maximum_fusion = bf16[2048,2048]{1,0:T(8,128)(2,1)} fusion(bf16[512,2048]{1,0:T(8,128)(2,1)S(1)} %bitcast.85, bf16[512,2048]{1,0:T(8,128)(2,1)S(1)} %bitcast.86, bf16[512,2048]{1,0:T(8,128)(2,1)S(1)} %bitcast.87, bf16[512,2048]{1,0:T(8,128)(2,1)S(1)} %bitcast.84), kind=kLoop, calls=%fused_computation | loop fusion | flops 33554432 | bytes 16777216 | tf_op jit(solution)/shard_map/concatenate | solution.py:85
  51.2 2.3 %select_dynamic-update-slice_fusion.4 = bf16[1160,2048]{1,0:T(8,128)(2,1)} fusion(bf16[136,2048]{1,0:T(8,128)(2,1)S(1)} %collective-permute-done, bf16[136,2048]{1,0:T(8,128)(2,1)} %collective-permute-done.1, bf16[136,2048]{1,0:T(8,128)(2,1)} %collective-permute-done.2, bf16[136,2048]{1,0:T(8,128)(2,1)} %collective-permute-done.3, pred[]{:T(512)S(6)} %eq.79, ...), kind=kLoop, calls=%fused_computation.44 | loop fusion | flops 1114111 | bytes 2785284
  53.5 1.7 select_dynamic-update-slice_fusion.3
  55.2 1.7 select_dynamic-update-slice_fusion.2
  56.9 1.7 select_dynamic-update-slice_fusion.1
  58.6 1.7 select_dynamic-update-slice_fusion
  60.3 80.1 %all-to-all-done = bf16[48,32,2048]{2,1,0:T(8,128)(2,1)} async-done(((bf16[48,32,2048]{2,1,0:T(8,128)(2,1)}), bf16[48,32,2048]{2,1,0:T(8,128)(2,1)}, u32[]{:S(2)}, u32[]{:S(2)}) %all-to-all-start) | async-done | bytes 6291488 | tf_op jit(solution)/shard_map/all_to_all | solution.py:70
  140.4 11.2 %convolution_convert_fusion = bf16[1160,1536]{1,0:T(8,128)(2,1)S(1)} fusion(bf16[1160,2048]{1,0:T(8,128)(2,1)} %select_dynamic-update-slice_fusion, bf16[1536,2048]{1,0:T(8,128)(2,1)} %bitcast.8), kind=kOutput, calls=%fused_computation.11 | convolution fusion | flops 7299870720 | bytes 14606336 | tf_op jit(solution)/shard_map/dot_general | solution.py:87
  151.6 10.7 %multiply_add_fusion = f32[1152,1536]{1,0:T(8,128)S(1)} fusion(bf16[1160,1536]{1,0:T(8,128)(2,1)S(1)} %convolution_convert_fusion, f32[1536]{0:T(1024)S(1)} %mul.115, f32[1536]{0:T(1024)S(1)} %mul.112, f32[1536]{0:T(1024)S(1)} %mul.109, f32[1536]{0:T(1024)S(1)} %mul.106, f32[1536]{0:T(1024)S(1)} %mul.103, f32[1536]{0:T(1024)S(1)} %mul.100, ...), kind=kLoop, calls=%fused_computation.12 | loop fusion | flops 47775744 | bytes 31901568 | tf_op jit(solution)/shard_map/add | solution.py:98
  162.3 2.9 %copy-done = f32[1152,1536]{1,0:T(8,128)} copy-done((f32[1152,1536]{1,0:T(8,128)}, f32[1152,1536]{1,0:T(8,128)S(1)}, u32[]{:S(2)}) %copy-start) | copy-done | bytes 7077912
  166.6 1.7 copy.20
  168.3 1.7 reshape.154
  170.0 2.3 %fusion.36 = (bf16[32,16,8,128]{3,2,1,0:T(8,128)(2,1)S(1)}, bf16[32,16,8,128]{3,2,1,0:T(8,128)(2,1)S(1)}) fusion(bf16[32,16,9,128]{3,2,1,0:T(8,128)(2,1)} %reshape.154), kind=kLoop, calls=%fused_computation.98 | loop fusion | bytes 4194304 | tf_op jit(solution)/shard_map/slice | solution.py:124
  172.3 5.8 %fusion = f32[32,8,128,16]{2,3,1,0:T(8,128)S(1)} fusion(pred[8,128,128]{2,1,0:T(8,128)(4,1)S(1)} %get-tuple-element.34, bf16[32,128,128]{2,1,0:T(8,128)(2,1)} %copy.22, bf16[32,16,8,128]{3,2,1,0:T(8,128)(2,1)S(1)} %get-tuple-element.14), kind=kOutput, calls=%fused_computation.1 | convolution fusion | flops 138412032 | bytes 4325376 | tf_op jit(solution)/shard_map/gcbj,bgij->gcbi/dot_general | solution.py:126
  178.1 4.5 %add_bitcast_fusion = f32[32,16,8,128]{3,1,2,0:T(8,128)S(1)} fusion(f32[32,8,128,16]{2,3,1,0:T(8,128)S(1)} %fusion, pred[8,128,128]{2,1,0:T(8,128)(4,1)S(1)} %get-tuple-element.33, bf16[32,128,128]{2,1,0:T(8,128)(2,1)S(1)} %copy-done.2, bf16[32,16,8,128]{3,2,1,0:T(8,128)(2,1)S(1)} %get-tuple-element.13), kind=kOutput, calls=%fused_computation.27 | convolution fusion | flops 138936320 | bytes 6422528 | tf_op jit(solution)/shard_map/gcbj,bgij->gcbi/dot_general | solution.py:123
  183.4 1.8 copy.35
  185.2 2.9 %copy.25 = f32[512,1024]{0,1:T(8,128)} copy(f32[512,1024]{1,0:T(8,128)} %bitcast.83) | data formatting | bytes 4194304 | tf_op jit(solution)/shard_map/reshape | solution.py:129
  188.1 2.6 %fusion.17 = bf16[512,1024]{0,1:T(8,128)(2,1)S(1)} fusion(f32[512,1024]{0,1:T(8,128)} %copy.25, f32[1152,1536]{1,0:T(8,128)} %copy-done), kind=kLoop, calls=%fused_computation.26 | loop fusion | flops 1048576 | bytes 5242880 | tf_op jit(solution)/shard_map/convert_element_type | solution.py:130
  190.8 1.4 collective-permute-start.7
  192.2 1.7 collective-permute-start.9
  193.9 6.1 %collective-permute-done.8 = bf16[256,512]{1,0:T(8,128)(2,1)S(1)} collective-permute-done((bf16[256,512]{1,0:T(8,128)(2,1)S(1)}, bf16[256,512]{1,0:T(8,128)(2,1)S(1)}, u32[]{:S(2)}, u32[]{:S(2)}) %collective-permute-start.8) | collective-permute-done | bytes 262176 | tf_op jit(solution)/shard_map/ppermute | solution.py:135
  200.1 5.8 %collective-permute-done.9 = bf16[256,512]{1,0:T(8,128)(2,1)S(1)} collective-permute-done((bf16[256,512]{1,0:T(8,128)(2,1)S(1)}, bf16[256,512]{1,0:T(8,128)(2,1)S(1)}, u32[]{:S(2)}, u32[]{:S(2)}) %collective-permute-start.9) | collective-permute-done | bytes 262176 | tf_op jit(solution)/shard_map/ppermute | solution.py:135
  205.9 6.7 %fusion.14 = bf16[256,2048]{1,0:T(8,128)(2,1)} fusion(bf16[2048,2048]{1,0:T(8,128)(2,1)} %pad_maximum_fusion, bf16[256,2048]{1,0:T(8,128)(2,1)S(1)} %copy-done.1, bf16[256,512]{1,0:T(8,128)(2,1)S(1)} %collective-permute-done.9, bf16[256,512]{1,0:T(8,128)(2,1)S(1)} %collective-permute-done.8, bf16[256,512]{1,0:T(8,128)(2,1)S(1)} %collective-permute-done.7, ...), kind=kOutput, calls=%fused_computation.20 | convolution fusion | flops 2153250816 | bytes 11534336 | tf_op jit(solution)/shard_map/dot_general | solution.py:137
  (66 shorter events, 22.3 us)
Async XLA Ops:
  1.9 44.1 %collective-permute-start = (bf16[136,2048]{1,0:T(8,128)(2,1)}, bf16[136,2048]{1,0:T(8,128)(2,1)S(1)}, u32[]{:S(2)}, u32[]{:S(2)}) collective-permute-start(bf16[136,2048]{1,0:T(8,128)(2,1)} %slice.75), channel_id=1, source_target_pairs={{3,7},{7,11},{11,15},{19,23},{23,27},{27,31},{35,39},{39,43},{43,4... | collective-permute-start | bytes 1671176 | tf_op jit(solution)/shard_map/ppermute | solution.py:56
  2.6 48.6 %collective-permute-start.1 = (bf16[136,2048]{1,0:T(8,128)(2,1)}, bf16[136,2048]{1,0:T(8,128)(2,1)}, u32[]{:S(2)}, u32[]{:S(2)}) collective-permute-start(bf16[136,2048]{1,0:T(8,128)(2,1)} %slice.75), channel_id=1, source_target_pairs={{3,6},{7,10},{11,14},{19,22},{23,26},{27,30},{35,38},{39,42},{43,4... | collective-permute-start | bytes 1671176 | tf_op jit(solution)/shard_map/ppermute | solution.py:56
  4.1 47.1 %collective-permute-start.2 = (bf16[136,2048]{1,0:T(8,128)(2,1)}, bf16[136,2048]{1,0:T(8,128)(2,1)}, u32[]{:S(2)}, u32[]{:S(2)}) collective-permute-start(bf16[136,2048]{1,0:T(8,128)(2,1)} %slice.75), channel_id=1, source_target_pairs={{3,5},{7,9},{11,13},{19,21},{23,25},{27,29},{35,37},{39,41},{43,45... | collective-permute-start | bytes 1671176 | tf_op jit(solution)/shard_map/ppermute | solution.py:56
  5.4 45.8 %collective-permute-start.3 = (bf16[136,2048]{1,0:T(8,128)(2,1)}, bf16[136,2048]{1,0:T(8,128)(2,1)}, u32[]{:S(2)}, u32[]{:S(2)}) collective-permute-start(bf16[136,2048]{1,0:T(8,128)(2,1)} %slice.75), channel_id=1, source_target_pairs={{3,4},{7,8},{11,12},{19,20},{23,24},{27,28},{35,36},{39,40},{43,44... | collective-permute-start | bytes 1671176 | tf_op jit(solution)/shard_map/ppermute | solution.py:56
  6.9 40.0 %collective-permute-start.4 = (bf16[256,2048]{1,0:T(8,128)(2,1)}, bf16[256,2048]{1,0:T(8,128)(2,1)S(1)}, u32[]{:S(2)}, u32[]{:S(2)}) collective-permute-start(bf16[256,2048]{1,0:T(8,128)(2,1)} %param.6), channel_id=1, source_target_pairs={{0,2},{1,3},{2,0},{3,1},{4,6},{5,7},{6,4},{7,5},{8,10},{9,11},{10,... | collective-permute-start | bytes 3145736 | tf_op jit(solution)/shard_map/ppermute | solution.py:43
  22.6 6.7 %copy-start.3 = (f32[7,6144]{1,0:T(8,128)S(1)}, f32[7,6144]{1,0:T(8,128)}, u32[]{:S(2)}) copy-start(f32[7,6144]{1,0:T(8,128)} %param.9) | copy-start | bytes 516100
  22.6 7.1 %copy-start.4 = (bf16[128,128]{1,0:T(8,128)(2,1)S(1)}, bf16[128,128]{1,0:T(8,128)(2,1)}, u32[]{:S(2)}) copy-start(bf16[128,128]{1,0:T(8,128)(2,1)} %param.10) | copy-start | bytes 98308
  22.6 7.7 %copy-start.5 = (s32[1,4]{1,0:T(1,128)S(1)}, s32[1,4]{1,0:T(1,128)}, u32[]{:S(2)}) copy-start(s32[1,4]{1,0:T(1,128)} %param.7) | copy-start | bytes 52
  22.6 117.8 %all-to-all-start = ((bf16[48,32,2048]{2,1,0:T(8,128)(2,1)}), bf16[48,32,2048]{2,1,0:T(8,128)(2,1)}, u32[]{:S(2)}, u32[]{:S(2)}) async-start(bf16[48,32,2048]{2,1,0:T(8,128)(2,1)} %constant_dynamic-update-slice_fusion), calls=%async_computation | async-start | bytes 12582912 | tf_op jit(solution)/shard_map/all_to_all | solution.py:70
  41.6 4.4 %copy-start.1 = (bf16[256,2048]{1,0:T(8,128)(2,1)S(1)}, bf16[256,2048]{1,0:T(8,128)(2,1)}, u32[]{:S(2)}) copy-start(bf16[256,2048]{1,0:T(8,128)(2,1)} %param.6) | copy-start | bytes 3145732
  46.0 7.5 %collective-permute-start.6 = (bf16[256,2048]{1,0:T(8,128)(2,1)S(1)}, bf16[256,2048]{1,0:T(8,128)(2,1)S(1)}, u32[]{:S(2)}, u32[]{:S(2)}) collective-permute-start(bf16[256,2048]{1,0:T(8,128)(2,1)S(1)} %copy-done.1), channel_id=1, source_target_pairs={{0,1},{1,0},{2,3},{3,2},{4,5},{5,4},{6,7},{7,6},{8,9},{9,8},{10,11... | collective-permute-start | bytes 3145736 | tf_op jit(solution)/shard_map/ppermute | solution.py:41
  46.9 6.7 %collective-permute-start.5 = (bf16[256,2048]{1,0:T(8,128)(2,1)S(1)}, bf16[256,2048]{1,0:T(8,128)(2,1)S(1)}, u32[]{:S(2)}, u32[]{:S(2)}) collective-permute-start(bf16[256,2048]{1,0:T(8,128)(2,1)S(1)} %collective-permute-done.4), channel_id=1, source_target_pairs={{0,1},{1,0},{2,3},{3,2},{4,5},{5,4},{6,7},{7,6},{8,9},{9,8},{10,11... | collective-permute-start | bytes 3145736 | tf_op jit(solution)/shard_map/ppermute | solution.py:44
  162.3 2.9 %copy-start = (f32[1152,1536]{1,0:T(8,128)}, f32[1152,1536]{1,0:T(8,128)S(1)}, u32[]{:S(2)}) copy-start(f32[1152,1536]{1,0:T(8,128)S(1)} %multiply_add_fusion) | copy-start | bytes 21233668
  172.3 5.8 %copy-start.2 = (bf16[32,128,128]{2,1,0:T(8,128)(2,1)S(1)}, bf16[32,128,128]{2,1,0:T(8,128)(2,1)}, u32[]{:S(2)}) copy-start(bf16[32,128,128]{2,1,0:T(8,128)(2,1)} %copy.19) | copy-start | bytes 3145732
  190.8 3.2 %collective-permute-start.7 = (bf16[256,512]{1,0:T(8,128)(2,1)S(1)}, bf16[256,512]{1,0:T(8,128)(2,1)S(1)}, u32[]{:S(2)}, u32[]{:S(2)}) collective-permute-start(bf16[256,512]{1,0:T(8,128)(2,1)S(1)} %get-tuple-element.18), channel_id=1, source_target_pairs={{0,1},{1,0},{2,3},{3,2},{4,5},{5,4},{6,7},{7,6},{8,9},{9,8},{10,11... | collective-permute-start | bytes 786440 | tf_op jit(solution)/shard_map/ppermute | solution.py:135
  192.2 7.9 %collective-permute-start.8 = (bf16[256,512]{1,0:T(8,128)(2,1)S(1)}, bf16[256,512]{1,0:T(8,128)(2,1)S(1)}, u32[]{:S(2)}, u32[]{:S(2)}) collective-permute-start(bf16[256,512]{1,0:T(8,128)(2,1)S(1)} %get-tuple-element.17), channel_id=1, source_target_pairs={{0,2},{1,3},{2,0},{3,1},{4,6},{5,7},{6,4},{7,5},{8,10},{9,11},{10,... | collective-permute-start | bytes 786440 | tf_op jit(solution)/shard_map/ppermute | solution.py:135
  192.2 13.7 %collective-permute-start.9 = (bf16[256,512]{1,0:T(8,128)(2,1)S(1)}, bf16[256,512]{1,0:T(8,128)(2,1)S(1)}, u32[]{:S(2)}, u32[]{:S(2)}) collective-permute-start(bf16[256,512]{1,0:T(8,128)(2,1)S(1)} %get-tuple-element.16), channel_id=1, source_target_pairs={{0,3},{1,2},{2,1},{3,0},{4,7},{5,6},{6,5},{7,4},{8,11},{9,10},{10,... | collective-permute-start | bytes 786440 | tf_op jit(solution)/shard_map/ppermute | solution.py:135
